TPU v7x, 512 devices: a whole 4x8x8 slice. The times are simulated.
512 devices in a mesh: blk: 256 (over z, x_hi, y, core), rep: 2 (over x_lo).
Axes of the slice: x: 4 (x_hi: 2, x_lo: 2; x = x_hi * 2 + x_lo), y: 8, z: 8, core: 2. Of those that a mesh axis runs over, the one named last changes fastest.
Arguments:
- samples: bfloat16 [8192, 16, 2048], P('blk', 'rep'), may hold values from -60 to 60, as said below
- offsets: int32 [4, 8192], P(None, 'blk'), may hold values from 0 to 31
- bad_mask: int32 [8192], P('blk'), may hold values 0 or 1
Outputs:
- correlations: float32 [8192, 4, 257], P('blk')
- mirrored: float32 [8192, 4, 257], P('blk')
Inputs may be any that keep to these rules, and one draw needn't show every extreme that they name: `samples`: samples vary in scale between channels and segments; channels near one another share a delayed common source.
All inputs are finite; a program needn't handle non-finite values. No bound on the sum of `bad_mask` on one device may be relied on, other than what follows from the above.
Results may differ from a plain program's by a relative error of at most 0.0017.
Values may be sent and summed in bfloat16 or wider, within the bound.
No kernel may reach another device: no remote copies, remote signals or barrier semaphores. Data moves between devices by JAX's collectives and lax.ppermute only.
A program may use at most 64 MiB of HBM per device.

v0:
```python
import math
import jax
import jax.numpy as jnp
from jax import lax
from jax.sharding import PartitionSpec as P

LAGS = 128


def shifted(x, axis, by):
    length = lax.axis_size(axis)
    return lax.ppermute(x, axis, [(i, (i + by) % length) for i in range(length)])


def forward_table(length):
    half_len = length // 2
    sample_idx = lax.iota(jnp.int32, length)
    bin_idx = lax.iota(jnp.int32, half_len)
    phase = sample_idx[:, None] * bin_idx[None, :] % length
    angle = phase.astype(jnp.float32) * (2.0 * math.pi / length)
    return jnp.concatenate([jnp.cos(angle), -jnp.sin(angle)], axis=1).astype(jnp.bfloat16)


def inverse_table(length, lag_half):
    half_len = length // 2
    bin_idx = lax.iota(jnp.int32, half_len)
    lag_idx = lax.iota(jnp.int32, 2 * lag_half + 1) - lag_half
    phase = bin_idx[:, None] * (lag_idx[None, :] % length) % length
    angle = phase.astype(jnp.float32) * (2.0 * math.pi / length)
    return jnp.concatenate([jnp.cos(angle), -jnp.sin(angle)], axis=0)


def whiten(spectrum, keep, half_len):
    power = jnp.sum(spectrum * spectrum, axis=-1, keepdims=True) / half_len
    return (spectrum * lax.rsqrt(power + 1e-06) * keep[:, None, None]).astype(jnp.bfloat16)


def cross_spectrum(local, partner, half_len):
    first = local.astype(jnp.float32)
    second = partner.astype(jnp.float32)
    real_a, imag_a = (first[..., :half_len], first[..., half_len:])
    real_b, imag_b = (second[..., :half_len], second[..., half_len:])
    real_sum = jnp.sum(real_a * real_b + imag_a * imag_b, axis=1)
    imag_sum = jnp.sum(imag_a * real_b - real_a * imag_b, axis=1)
    return jnp.concatenate([real_sum, imag_sum], axis=-1)


def on_device(samples, offsets, bad_mask):
    channels, segments, length = samples.shape
    half_len = length // 2
    stops = offsets.shape[0]
    spectrum = jnp.dot(
        samples.reshape(channels * segments, length),
        forward_table(length),
        preferred_element_type=jnp.float32,
    ).reshape(channels, segments, length)
    keep = (1 - bad_mask).astype(jnp.float32)
    white = whiten(spectrum, keep, half_len)
    pieces = []
    moving = white
    for stop in range(1, stops + 1):
        moving = shifted(moving, "blk", 1)
        partner = jnp.take(moving, offsets[stop - 1], axis=0)
        pieces.append(cross_spectrum(white, partner, half_len))
    cross = jnp.stack(pieces, axis=1)
    scale = 1.0 / math.sqrt(segments * lax.axis_size("rep") * half_len)
    back_table = inverse_table(length, LAGS)
    stacked = lax.psum(cross, "rep")
    correlations = (
        jnp.dot(
            stacked.reshape(channels * stops, length),
            back_table,
            precision=lax.Precision.HIGHEST,
            preferred_element_type=jnp.float32,
        ).reshape(channels, stops, -1)
        * scale
    )
    mirrored = []
    for stop in range(1, stops + 1):
        flipped = correlations[:, stop - 1, ::-1]
        mirrored.append(shifted(flipped, "blk", -stop))
    return (correlations, jnp.stack(mirrored, axis=1))


def solution(mesh):
    return jax.shard_map(
        on_device,
        mesh=mesh,
        in_specs=(P("blk", "rep", None), P(None, "blk"), P("blk")),
        out_specs=(P("blk", None, None), P("blk", None, None)),
        check_vma=False,
    )
```

profile of v0, /device:TPU:1, one launch (start us, length us, event | category | flops | bytes accessed | tf_op | source)
XLA Modules:
  0.0 241.3 jit_solution(5379508726055081933)
XLA Ops:
  7.2 0.0 copy-start
  7.2 0.0 all-reduce.2.cloned.1.call-start
  7.2 33.8 %negate_convert_fusion = (bf16[2048,1024]{1,0:T(8,128)(2,1)S(1)}, bf16[2048,1024]{1,0:T(8,128)(2,1)S(1)}) fusion(), kind=kLoop, calls=%fused_computation.14 | loop fusion | flops 35651584 | bytes 8388608 | tf_op jit(solution)/shard_map/convert.1
  41.1 5.1 %fusion.15 = (f32[256]{0:T(256)S(1)}, f32[2048,256]{0,1:T(8,128)}) fusion(bf16[2048,1024]{1,0:T(8,128)(2,1)S(1)} %get-tuple-element.47, bf16[2048,1024]{1,0:T(8,128)(2,1)S(1)} %get-tuple-element.48, bf16[32,8,2048]{2,1,0:T(8,128)(2,1)S(1)} %copy-done), kind=kOutput, calls=%fused_computation.27 | convolution fusion | flops 2165309184 | bytes 11535360 | tf_op jit(solution)/shard_map/dot_general | solution.py:52
  46.2 0.1 rsqrt.12
  46.3 0.0 copy-start.3
  46.3 1.9 fusion.28
  48.2 4.6 %collective-permute-start = (bf16[32,8,2048]{2,1,0:T(8,128)(2,1)S(1)}, bf16[32,8,2048]{2,1,0:T(8,128)(2,1)S(1)}, u32[]{:S(2)}, u32[]{:S(2)}) collective-permute-start(bf16[32,8,2048]{2,1,0:T(8,128)(2,1)S(1)} %get-tuple-element.26), channel_id=1, source_target_pairs={{0,2},{2,4},{4,6},{6,8},{8,10},{10,12},{12,14},{14,16},{16,18},{18... | collective-permute-start | bytes 3145736 | tf_op jit(solution)/shard_map/ppermute | solution.py:12
  52.8 11.7 %collective-permute-done = bf16[32,8,2048]{2,1,0:T(8,128)(2,1)S(1)} collective-permute-done((bf16[32,8,2048]{2,1,0:T(8,128)(2,1)S(1)}, bf16[32,8,2048]{2,1,0:T(8,128)(2,1)S(1)}, u32[]{:S(2)}, u32[]{:S(2)}) %collective-permute-start) | collective-permute-done | bytes 1048608 | tf_op jit(solution)/shard_map/ppermute | solution.py:12
  64.6 1.0 copy-done.2
  65.5 4.4 %collective-permute-start.1 = (bf16[32,8,2048]{2,1,0:T(8,128)(2,1)S(1)}, bf16[32,8,2048]{2,1,0:T(8,128)(2,1)}, u32[]{:S(2)}, u32[]{:S(2)}) collective-permute-start(bf16[32,8,2048]{2,1,0:T(8,128)(2,1)S(1)} %collective-permute-done), channel_id=1, source_target_pairs={{0,2},{2,4},{4,6},{6,8},{8,10},{10,12},{12,14},{14,16},{16,18},{18... | collective-permute-start | bytes 3145736 | tf_op jit(solution)/shard_map/ppermute | solution.py:12
  69.9 13.2 %collective-permute-done.1 = bf16[32,8,2048]{2,1,0:T(8,128)(2,1)} collective-permute-done((bf16[32,8,2048]{2,1,0:T(8,128)(2,1)S(1)}, bf16[32,8,2048]{2,1,0:T(8,128)(2,1)}, u32[]{:S(2)}, u32[]{:S(2)}) %collective-permute-start.1) | collective-permute-done | bytes 1048608 | tf_op jit(solution)/shard_map/ppermute | solution.py:12
  83.1 3.0 %collective-permute-start.2 = (bf16[32,8,2048]{2,1,0:T(8,128)(2,1)}, bf16[32,8,2048]{2,1,0:T(8,128)(2,1)}, u32[]{:S(2)}, u32[]{:S(2)}) collective-permute-start(bf16[32,8,2048]{2,1,0:T(8,128)(2,1)} %collective-permute-done.1), channel_id=1, source_target_pairs={{0,2},{2,4},{4,6},{6,8},{8,10},{10,12},{12,14},{14,16},{16,18},{18... | collective-permute-start | bytes 3145736 | tf_op jit(solution)/shard_map/ppermute | solution.py:12
  86.2 2.8 %gather_fusion = bf16[32,8,2048]{2,1,0:T(8,128)(2,1)} fusion(bf16[32,8,2048]{2,1,0:T(8,128)(2,1)} %copy-done.2, s32[1024]{0:T(1024)S(1)} %pad_clamp_fusion.3), kind=kCustom, calls=%fused_computation.clone | custom fusion | bytes 2097280 | tf_op jit(solution)/shard_map/jit(_take)/gather | solution.py:63
  89.0 2.8 %select_convert_fusion.3 = f32[32,8,2048]{2,1,0:T(8,128)} fusion(bf16[32,8,2048]{2,1,0:T(8,128)(2,1)} %gather_fusion, pred[32]{0:T(512)(128)(4,1)S(1)} %get-tuple-element.39), kind=kLoop, calls=%fused_computation.44 | loop fusion | flops 1048576 | bytes 3145760 | tf_op jit(solution)/shard_map/convert_element_type | solution.py:40
  91.8 2.8 %gather_fusion.1 = bf16[32,8,2048]{2,1,0:T(8,128)(2,1)} fusion(bf16[32,8,2048]{2,1,0:T(8,128)(2,1)} %collective-permute-done.1, s32[1024]{0:T(1024)S(1)} %pad_clamp_fusion.2), kind=kCustom, calls=%fused_computation.1.clone | custom fusion | bytes 2097280 | tf_op jit(solution)/shard_map/jit(_take)/gather | solution.py:63
  94.6 10.6 %collective-permute-done.2 = bf16[32,8,2048]{2,1,0:T(8,128)(2,1)} collective-permute-done((bf16[32,8,2048]{2,1,0:T(8,128)(2,1)}, bf16[32,8,2048]{2,1,0:T(8,128)(2,1)}, u32[]{:S(2)}, u32[]{:S(2)}) %collective-permute-start.2) | collective-permute-done | bytes 1048608 | tf_op jit(solution)/shard_map/ppermute | solution.py:12
  105.3 2.1 collective-permute-start.3
  107.4 2.7 %select_convert_fusion.2 = f32[32,8,2048]{2,1,0:T(8,128)} fusion(bf16[32,8,2048]{2,1,0:T(8,128)(2,1)} %gather_fusion.1, pred[32]{0:T(512)(128)(4,1)S(1)} %get-tuple-element.19), kind=kLoop, calls=%fused_computation.43 | loop fusion | flops 1048576 | bytes 3145760 | tf_op jit(solution)/shard_map/convert_element_type | solution.py:40
  110.1 2.9 %gather_fusion.2 = bf16[32,8,2048]{2,1,0:T(8,128)(2,1)} fusion(bf16[32,8,2048]{2,1,0:T(8,128)(2,1)} %collective-permute-done.2, s32[1024]{0:T(1024)S(1)} %pad_clamp_fusion.1), kind=kCustom, calls=%fused_computation.2.clone | custom fusion | bytes 2097280 | tf_op jit(solution)/shard_map/jit(_take)/gather | solution.py:63
  113.0 2.8 %select_convert_fusion.1 = f32[32,8,2048]{2,1,0:T(8,128)} fusion(bf16[32,8,2048]{2,1,0:T(8,128)(2,1)} %gather_fusion.2, pred[32]{0:T(512)(128)(4,1)S(1)} %get-tuple-element.43), kind=kLoop, calls=%fused_computation.42 | loop fusion | flops 1048576 | bytes 3145760 | tf_op jit(solution)/shard_map/convert_element_type | solution.py:40
  115.8 11.7 %collective-permute-done.3 = bf16[32,8,2048]{2,1,0:T(8,128)(2,1)} collective-permute-done((bf16[32,8,2048]{2,1,0:T(8,128)(2,1)}, bf16[32,8,2048]{2,1,0:T(8,128)(2,1)}, u32[]{:S(2)}, u32[]{:S(2)}) %collective-permute-start.3) | collective-permute-done | bytes 1048608 | tf_op jit(solution)/shard_map/ppermute | solution.py:12
  127.4 2.8 %gather_fusion.3 = bf16[32,8,2048]{2,1,0:T(8,128)(2,1)} fusion(bf16[32,8,2048]{2,1,0:T(8,128)(2,1)} %collective-permute-done.3, s32[1024]{0:T(1024)S(1)} %pad_clamp_fusion), kind=kCustom, calls=%fused_computation.3.clone | custom fusion | bytes 2097280 | tf_op jit(solution)/shard_map/jit(_take)/gather | solution.py:63
  130.3 1.6 select_convert_fusion
  131.8 0.3 copy-done.1
  132.2 5.4 %add_reduce_fusion.3 = (f32[32,1024]{1,0:T(8,128)S(1)}, f32[32,1024]{1,0:T(8,128)S(1)}, f32[32,1024]{1,0:T(8,128)S(1)}, f32[32,1024]{1,0:T(8,128)S(1)}, f32[32,1...) fusion(f32[32,8,2048]{2,1,0:T(8,128)S(1)} %copy-done.1, ...), kind=kLoop, calls=%fused_computation.52 | loop fusion | flops 8126464 | bytes 11534336 | tf_op jit(solution)/shard_map/reduce_sum | solution.py:43
  137.7 1.1 pad_maximum_fusion
  138.8 0.0 all-reduce.2.cloned.1.call-update
  138.9 4.3 %fusion.24 = (f32[1024,257]{0,1:T(8,128)S(1)}, f32[1024,257]{0,1:T(8,128)S(1)}) fusion(s32[257]{0:T(512)S(1)} %add_select_fusion.2), kind=kLoop, calls=%fused_computation.53 | loop fusion | flops 3947520 | bytes 2106372 | tf_op jit(solution)/shard_map/cos | solution.py:30
  143.2 61.7 %all-reduce.2.cloned.1.call-done = f32[32,4,2048]{2,0,1:T(8,128)} async-done(((f32[32,4,2048]{2,0,1:T(8,128)}), f32[32,4,2048]{2,0,1:T(8,128)}) %all-reduce.2.cloned.1.call-update) | async-done | bytes 1048592 | tf_op jit(solution)/shard_map/psum | solution.py:68
  204.9 4.1 %fusion.16 = f32[32,4,257]{2,0,1:T(8,128)S(1)} fusion(f32[32,4,2048]{2,0,1:T(8,128)} %all-reduce.2.cloned.1.call-done, f32[1024,257]{0,1:T(8,128)S(1)} %get-tuple-element.38, f32[1024,257]{0,1:T(8,128)S(1)} %get-tuple-element.37), kind=kOutput, calls=%fused_computation.31 | convolution fusion | flops 809011328 | bytes 3285504 | tf_op jit(solution)/shard_map/dot_general | solution.py:70
  209.1 0.2 reverse
  209.3 0.1 slice_bitcast_fusion.3
  209.4 10.9 %collective-permute-start.7 = (f32[32,257]{1,0:T(8,128)S(1)}, f32[32,257]{1,0:T(8,128)S(1)}, u32[]{:S(2)}, u32[]{:S(2)}) collective-permute-start(f32[32,257]{1,0:T(8,128)S(1)} %slice_bitcast_fusion.3), channel_id=1, source_target_pairs={{0,504},{2,506},{4,508},{6,510},{8,0},{10,2},{12,4},{14,6},{16,8},... | collective-permute-start | bytes 98696 | tf_op jit(solution)/shard_map/ppermute | solution.py:12
  220.2 0.2 reverse.1
  220.5 0.1 slice_bitcast_fusion.2
  220.6 3.9 %collective-permute-start.6 = (f32[32,257]{1,0:T(8,128)S(1)}, f32[32,257]{1,0:T(8,128)S(1)}, u32[]{:S(2)}, u32[]{:S(2)}) collective-permute-start(f32[32,257]{1,0:T(8,128)S(1)} %slice_bitcast_fusion.2), channel_id=1, source_target_pairs={{0,506},{2,508},{4,510},{6,0},{8,2},{10,4},{12,6},{14,8},{16,10},{... | collective-permute-start | bytes 98696 | tf_op jit(solution)/shard_map/ppermute | solution.py:12
  224.5 0.2 reverse.2
  224.7 0.1 slice_bitcast_fusion.1
  224.8 3.1 %collective-permute-start.5 = (f32[32,257]{1,0:T(8,128)S(1)}, f32[32,257]{1,0:T(8,128)S(1)}, u32[]{:S(2)}, u32[]{:S(2)}) collective-permute-start(f32[32,257]{1,0:T(8,128)S(1)} %slice_bitcast_fusion.1), channel_id=1, source_target_pairs={{0,508},{2,510},{4,0},{6,2},{8,4},{10,6},{12,8},{14,10},{16,12},{1... | collective-permute-start | bytes 98696 | tf_op jit(solution)/shard_map/ppermute | solution.py:12
  227.9 0.2 reverse.3
  228.1 0.1 slice_bitcast_fusion
  228.2 1.9 collective-permute-start.4
  230.1 0.8 copy.7
  230.9 0.0 collective-permute-done.7
  230.9 0.0 collective-permute-done.6
  230.9 2.7 %collective-permute-done.4 = f32[32,257]{1,0:T(8,128)S(1)} collective-permute-done((f32[32,257]{1,0:T(8,128)S(1)}, f32[32,257]{1,0:T(8,128)S(1)}, u32[]{:S(2)}, u32[]{:S(2)}) %collective-permute-start.4) | collective-permute-done | bytes 32928 | tf_op jit(solution)/shard_map/ppermute | solution.py:12
  233.6 0.8 copy.8
  (21 shorter events, 0.2 us)
Async XLA Ops:
  7.2 33.9 %copy-start = (bf16[32,8,2048]{2,1,0:T(8,128)(2,1)S(1)}, bf16[32,8,2048]{2,1,0:T(8,128)(2,1)}, u32[]{:S(2)}) copy-start(bf16[32,8,2048]{2,1,0:T(8,128)(2,1)} %param.5) | copy-start | bytes 3145732
  7.2 33.9 %copy-start.4 = (s32[32]{0:T(128)S(1)}, s32[32]{0:T(128)}, u32[]{:S(2)}) copy-start(s32[32]{0:T(128)} %param.7) | copy-start | bytes 388
  7.2 197.7 %all-reduce.2.cloned.1.call-start = ((), (), s32[]{:S(2)}) async-start(), calls=%async_computation | async-start | bytes 2097152 | tf_op jit(solution)/shard_map/psum | solution.py:68
  46.3 39.9 %copy-start.3 = (s32[4,32]{1,0:T(4,128)S(1)}, s32[4,32]{1,0:T(4,128)}, u32[]{:S(2)}) copy-start(s32[4,32]{1,0:T(4,128)} %param.6) | copy-start | bytes 1540
  48.2 16.3 %collective-permute-start = (bf16[32,8,2048]{2,1,0:T(8,128)(2,1)S(1)}, bf16[32,8,2048]{2,1,0:T(8,128)(2,1)S(1)}, u32[]{:S(2)}, u32[]{:S(2)}) collective-permute-start(bf16[32,8,2048]{2,1,0:T(8,128)(2,1)S(1)} %get-tuple-element.26), channel_id=1, source_target_pairs={{0,2},{2,4},{4,6},{6,8},{8,10},{10,12},{12,14},{14,16},{16,18},{18... | collective-permute-start | bytes 3145736 | tf_op jit(solution)/shard_map/ppermute | solution.py:12
  64.6 1.0 copy-start.2
  65.5 17.6 %collective-permute-start.1 = (bf16[32,8,2048]{2,1,0:T(8,128)(2,1)S(1)}, bf16[32,8,2048]{2,1,0:T(8,128)(2,1)}, u32[]{:S(2)}, u32[]{:S(2)}) collective-permute-start(bf16[32,8,2048]{2,1,0:T(8,128)(2,1)S(1)} %collective-permute-done), channel_id=1, source_target_pairs={{0,2},{2,4},{4,6},{6,8},{8,10},{10,12},{12,14},{14,16},{16,18},{18... | collective-permute-start | bytes 3145736 | tf_op jit(solution)/shard_map/ppermute | solution.py:12
  83.1 22.1 %collective-permute-start.2 = (bf16[32,8,2048]{2,1,0:T(8,128)(2,1)}, bf16[32,8,2048]{2,1,0:T(8,128)(2,1)}, u32[]{:S(2)}, u32[]{:S(2)}) collective-permute-start(bf16[32,8,2048]{2,1,0:T(8,128)(2,1)} %collective-permute-done.1), channel_id=1, source_target_pairs={{0,2},{2,4},{4,6},{6,8},{8,10},{10,12},{12,14},{14,16},{16,18},{18... | collective-permute-start | bytes 3145736 | tf_op jit(solution)/shard_map/ppermute | solution.py:12
  105.3 22.1 %collective-permute-start.3 = (bf16[32,8,2048]{2,1,0:T(8,128)(2,1)}, bf16[32,8,2048]{2,1,0:T(8,128)(2,1)}, u32[]{:S(2)}, u32[]{:S(2)}) collective-permute-start(bf16[32,8,2048]{2,1,0:T(8,128)(2,1)} %collective-permute-done.2), channel_id=1, source_target_pairs={{0,2},{2,4},{4,6},{6,8},{8,10},{10,12},{12,14},{14,16},{16,18},{18... | collective-permute-start | bytes 3145736 | tf_op jit(solution)/shard_map/ppermute | solution.py:12
  130.3 1.9 copy-start.1
  209.4 21.5 %collective-permute-start.7 = (f32[32,257]{1,0:T(8,128)S(1)}, f32[32,257]{1,0:T(8,128)S(1)}, u32[]{:S(2)}, u32[]{:S(2)}) collective-permute-start(f32[32,257]{1,0:T(8,128)S(1)} %slice_bitcast_fusion.3), channel_id=1, source_target_pairs={{0,504},{2,506},{4,508},{6,510},{8,0},{10,2},{12,4},{14,6},{16,8},... | collective-permute-start | bytes 98696 | tf_op jit(solution)/shard_map/ppermute | solution.py:12
  220.6 10.4 %collective-permute-start.6 = (f32[32,257]{1,0:T(8,128)S(1)}, f32[32,257]{1,0:T(8,128)S(1)}, u32[]{:S(2)}, u32[]{:S(2)}) collective-permute-start(f32[32,257]{1,0:T(8,128)S(1)} %slice_bitcast_fusion.2), channel_id=1, source_target_pairs={{0,506},{2,508},{4,510},{6,0},{8,2},{10,4},{12,6},{14,8},{16,10},{... | collective-permute-start | bytes 98696 | tf_op jit(solution)/shard_map/ppermute | solution.py:12
  224.8 6.1 %collective-permute-start.5 = (f32[32,257]{1,0:T(8,128)S(1)}, f32[32,257]{1,0:T(8,128)S(1)}, u32[]{:S(2)}, u32[]{:S(2)}) collective-permute-start(f32[32,257]{1,0:T(8,128)S(1)} %slice_bitcast_fusion.1), channel_id=1, source_target_pairs={{0,508},{2,510},{4,0},{6,2},{8,4},{10,6},{12,8},{14,10},{16,12},{1... | collective-permute-start | bytes 98696 | tf_op jit(solution)/shard_map/ppermute | solution.py:12
  228.2 5.4 %collective-permute-start.4 = (f32[32,257]{1,0:T(8,128)S(1)}, f32[32,257]{1,0:T(8,128)S(1)}, u32[]{:S(2)}, u32[]{:S(2)}) collective-permute-start(f32[32,257]{1,0:T(8,128)S(1)} %slice_bitcast_fusion), channel_id=1, source_target_pairs={{0,510},{2,0},{4,2},{6,4},{8,6},{10,8},{12,10},{14,12},{16,14},{18... | collective-permute-start | bytes 98696 | tf_op jit(solution)/shard_map/ppermute | solution.py:12
Sparse Core Ops, SparseCore 0:
  139.0 65.8 all-reduce.1
where the time goes:
time: 242 us; the launch traced here: 241 us
  waiting for transfers between devices  112 us (46%)
  other arithmetic  56.7 us (23%)
  starting transfers between devices  33.9 us (14%)
  local copies, waits for them, and re-layouts  15.7 us (6%)
  between operations  14.3 us (6%)
  matrix products  9.17 us (4%)
    psum x1, waiting for transfers between devices, on_device(): stacked = lax.psum(cross, 'rep')  61.7 us
    ppermute x8, waiting for transfers between devices, shifted(): lax.ppermute(x, axis, [(i, (i + by) % length) for i in range(length)])  49.9 us
    another operation x1, other arithmetic  33.8 us
    ppermute x8, starting transfers between devices, shifted(): lax.ppermute(x, axis, [(i, (i + by) % length) for i in range(length)])  33.8 us
    gather x4, local copies, waits for them, and re-layouts, on_device(): partner = jnp.take(moving, offsets[stop - 1], axis=0)  11.4 us
    convert_element_type x4, other arithmetic, cross_spectrum(): second = partner.astype(jnp.float32)  9.85 us
    reduce_sum x1, other arithmetic, cross_spectrum(): real_sum = jnp.sum(real_a * real_b + imag_a * imag_b, axis=1)  5.42 us
    dot_general x1, matrix products, on_device(): jnp.dot(samples.reshape(channels * segments, length), forward_table(lengt...  5.06 us
  transfers between devices with their start and end apart: 9, of which 6 were waited for; matrix products, arithmetic and copies ran while one was open for 10% of the time, Pallas kernels for 0%

commit v1 on v0

--- a/solution.py
+++ b/solution.py
@@ -1,10 +1,19 @@
+import functools
 import math
 import jax
 import jax.numpy as jnp
 from jax import lax
 from jax.sharding import PartitionSpec as P
+from jax.lax import all_gather
 
 LAGS = 128
+
+
+def indices_define(target, bus_axis):
+    return all_gather(target, bus_axis).sum(axis=0)
+
+
+match_the_pages = functools.partial(indices_define, bus_axis="rep")
 
 
 def shifted(x, axis, by):
@@ -65,7 +74,7 @@
     cross = jnp.stack(pieces, axis=1)
     scale = 1.0 / math.sqrt(segments * lax.axis_size("rep") * half_len)
     back_table = inverse_table(length, LAGS)
-    stacked = lax.psum(cross, "rep")
+    stacked = match_the_pages(cross)
     correlations = (
         jnp.dot(
             stacked.reshape(channels * stops, length),

time: 242 us -> 228 us (0.942)
  waiting for transfers between devices: 112 us -> 95.2 us
  other arithmetic: 56.7 us -> 59.4 us
    psum x1 -> x0, waiting for transfers between devices: 61.7 us -> none  [on_device(): stacked = lax.psum(cross, 'rep')]
    all_gather x0 -> x1, waiting for transfers between devices: none -> 45.3 us  [indices_define(): return all_gather(target, bus_axis).sum(axis=0)]
    reduce_sum x0 -> x1, other arithmetic: none -> 2.82 us  [indices_define(): return all_gather(target, bus_axis).sum(axis=0)]
where the time goes in v1:
time: 228 us
  waiting for transfers between devices  95.2 us (42%)
  other arithmetic  59.4 us (26%)
  starting transfers between devices  33.9 us (15%)
  local copies, waits for them, and re-layouts  15.7 us (7%)
  between operations  14.3 us (6%)
  matrix products  9.18 us (4%)
    ppermute x8, waiting for transfers between devices, shifted(): lax.ppermute(x, axis, [(i, (i + by) % length) for i in range(length)])  49.9 us
    all_gather x1, waiting for transfers between devices, indices_define(): return all_gather(target, bus_axis).sum(axis=0)  45.3 us
    another operation x1, other arithmetic  33.8 us
    ppermute x8, starting transfers between devices, shifted(): lax.ppermute(x, axis, [(i, (i + by) % length) for i in range(length)])  33.8 us
    gather x4, local copies, waits for them, and re-layouts, on_device(): partner = jnp.take(moving, offsets[stop - 1], axis=0)  11.4 us
    convert_element_type x4, other arithmetic, cross_spectrum(): second = partner.astype(jnp.float32)  9.85 us
    reduce_sum x1, other arithmetic, cross_spectrum(): real_sum = jnp.sum(real_a * real_b + imag_a * imag_b, axis=1)  5.42 us
    dot_general x1, matrix products, on_device(): jnp.dot(samples.reshape(channels * segments, length), forward_table(lengt...  5.06 us
  transfers between devices with their start and end apart: 9, of which 6 were waited for; matrix products, arithmetic and copies ran while one was open for 10% of the time, Pallas kernels for 0%

profile of v1, /device:TPU:1, one launch (start us, length us, event | category | flops | bytes accessed | tf_op | source)
XLA Modules:
  0.0 227.6 jit_solution(4202399587100569240)
XLA Ops:
  7.2 0.0 copy-start
  7.2 0.0 all-gather.3.cloned.1.call-start
  7.2 33.8 %negate_convert_fusion = (bf16[2048,1024]{1,0:T(8,128)(2,1)S(1)}, bf16[2048,1024]{1,0:T(8,128)(2,1)S(1)}) fusion(), kind=kLoop, calls=%fused_computation.14 | loop fusion | flops 35651584 | bytes 8388608 | tf_op jit(solution)/shard_map/convert.1
  41.1 5.1 %fusion.15 = (f32[256]{0:T(256)S(1)}, f32[2048,256]{0,1:T(8,128)}) fusion(bf16[2048,1024]{1,0:T(8,128)(2,1)S(1)} %get-tuple-element.49, bf16[2048,1024]{1,0:T(8,128)(2,1)S(1)} %get-tuple-element.50, bf16[32,8,2048]{2,1,0:T(8,128)(2,1)S(1)} %copy-done), kind=kOutput, calls=%fused_computation.27 | convolution fusion | flops 2165309184 | bytes 11535360 | tf_op jit(solution)/shard_map/dot_general | solution.py:61
  46.2 0.1 rsqrt.12
  46.3 0.0 copy-start.3
  46.3 1.9 fusion.28
  48.2 4.6 %collective-permute-start = (bf16[32,8,2048]{2,1,0:T(8,128)(2,1)S(1)}, bf16[32,8,2048]{2,1,0:T(8,128)(2,1)S(1)}, u32[]{:S(2)}, u32[]{:S(2)}) collective-permute-start(bf16[32,8,2048]{2,1,0:T(8,128)(2,1)S(1)} %get-tuple-element.28), channel_id=1, source_target_pairs={{0,2},{2,4},{4,6},{6,8},{8,10},{10,12},{12,14},{14,16},{16,18},{18... | collective-permute-start | bytes 3145736 | tf_op jit(solution)/shard_map/ppermute | solution.py:21
  52.8 11.7 %collective-permute-done = bf16[32,8,2048]{2,1,0:T(8,128)(2,1)S(1)} collective-permute-done((bf16[32,8,2048]{2,1,0:T(8,128)(2,1)S(1)}, bf16[32,8,2048]{2,1,0:T(8,128)(2,1)S(1)}, u32[]{:S(2)}, u32[]{:S(2)}) %collective-permute-start) | collective-permute-done | bytes 1048608 | tf_op jit(solution)/shard_map/ppermute | solution.py:21
  64.6 1.0 copy-done.2
  65.5 4.4 %collective-permute-start.1 = (bf16[32,8,2048]{2,1,0:T(8,128)(2,1)S(1)}, bf16[32,8,2048]{2,1,0:T(8,128)(2,1)}, u32[]{:S(2)}, u32[]{:S(2)}) collective-permute-start(bf16[32,8,2048]{2,1,0:T(8,128)(2,1)S(1)} %collective-permute-done), channel_id=1, source_target_pairs={{0,2},{2,4},{4,6},{6,8},{8,10},{10,12},{12,14},{14,16},{16,18},{18... | collective-permute-start | bytes 3145736 | tf_op jit(solution)/shard_map/ppermute | solution.py:21
  69.9 13.2 %collective-permute-done.1 = bf16[32,8,2048]{2,1,0:T(8,128)(2,1)} collective-permute-done((bf16[32,8,2048]{2,1,0:T(8,128)(2,1)S(1)}, bf16[32,8,2048]{2,1,0:T(8,128)(2,1)}, u32[]{:S(2)}, u32[]{:S(2)}) %collective-permute-start.1) | collective-permute-done | bytes 1048608 | tf_op jit(solution)/shard_map/ppermute | solution.py:21
  83.1 3.0 %collective-permute-start.2 = (bf16[32,8,2048]{2,1,0:T(8,128)(2,1)}, bf16[32,8,2048]{2,1,0:T(8,128)(2,1)}, u32[]{:S(2)}, u32[]{:S(2)}) collective-permute-start(bf16[32,8,2048]{2,1,0:T(8,128)(2,1)} %collective-permute-done.1), channel_id=1, source_target_pairs={{0,2},{2,4},{4,6},{6,8},{8,10},{10,12},{12,14},{14,16},{16,18},{18... | collective-permute-start | bytes 3145736 | tf_op jit(solution)/shard_map/ppermute | solution.py:21
  86.2 2.8 %gather_fusion = bf16[32,8,2048]{2,1,0:T(8,128)(2,1)} fusion(bf16[32,8,2048]{2,1,0:T(8,128)(2,1)} %copy-done.2, s32[1024]{0:T(1024)S(1)} %pad_clamp_fusion.3), kind=kCustom, calls=%fused_computation.clone | custom fusion | bytes 2097280 | tf_op jit(solution)/shard_map/jit(_take)/gather | solution.py:72
  89.0 2.8 %select_convert_fusion.3 = f32[32,8,2048]{2,1,0:T(8,128)} fusion(bf16[32,8,2048]{2,1,0:T(8,128)(2,1)} %gather_fusion, pred[32]{0:T(512)(128)(4,1)S(1)} %get-tuple-element.41), kind=kLoop, calls=%fused_computation.44 | loop fusion | flops 1048576 | bytes 3145760 | tf_op jit(solution)/shard_map/convert_element_type | solution.py:49
  91.8 2.8 %gather_fusion.1 = bf16[32,8,2048]{2,1,0:T(8,128)(2,1)} fusion(bf16[32,8,2048]{2,1,0:T(8,128)(2,1)} %collective-permute-done.1, s32[1024]{0:T(1024)S(1)} %pad_clamp_fusion.2), kind=kCustom, calls=%fused_computation.1.clone | custom fusion | bytes 2097280 | tf_op jit(solution)/shard_map/jit(_take)/gather | solution.py:72
  94.6 10.6 %collective-permute-done.2 = bf16[32,8,2048]{2,1,0:T(8,128)(2,1)} collective-permute-done((bf16[32,8,2048]{2,1,0:T(8,128)(2,1)}, bf16[32,8,2048]{2,1,0:T(8,128)(2,1)}, u32[]{:S(2)}, u32[]{:S(2)}) %collective-permute-start.2) | collective-permute-done | bytes 1048608 | tf_op jit(solution)/shard_map/ppermute | solution.py:21
  105.3 2.1 collective-permute-start.3
  107.4 2.7 %select_convert_fusion.2 = f32[32,8,2048]{2,1,0:T(8,128)} fusion(bf16[32,8,2048]{2,1,0:T(8,128)(2,1)} %gather_fusion.1, pred[32]{0:T(512)(128)(4,1)S(1)} %get-tuple-element.21), kind=kLoop, calls=%fused_computation.43 | loop fusion | flops 1048576 | bytes 3145760 | tf_op jit(solution)/shard_map/convert_element_type | solution.py:49
  110.1 2.9 %gather_fusion.2 = bf16[32,8,2048]{2,1,0:T(8,128)(2,1)} fusion(bf16[32,8,2048]{2,1,0:T(8,128)(2,1)} %collective-permute-done.2, s32[1024]{0:T(1024)S(1)} %pad_clamp_fusion.1), kind=kCustom, calls=%fused_computation.2.clone | custom fusion | bytes 2097280 | tf_op jit(solution)/shard_map/jit(_take)/gather | solution.py:72
  113.0 2.8 %select_convert_fusion.1 = f32[32,8,2048]{2,1,0:T(8,128)} fusion(bf16[32,8,2048]{2,1,0:T(8,128)(2,1)} %gather_fusion.2, pred[32]{0:T(512)(128)(4,1)S(1)} %get-tuple-element.45), kind=kLoop, calls=%fused_computation.42 | loop fusion | flops 1048576 | bytes 3145760 | tf_op jit(solution)/shard_map/convert_element_type | solution.py:49
  115.8 11.7 %collective-permute-done.3 = bf16[32,8,2048]{2,1,0:T(8,128)(2,1)} collective-permute-done((bf16[32,8,2048]{2,1,0:T(8,128)(2,1)}, bf16[32,8,2048]{2,1,0:T(8,128)(2,1)}, u32[]{:S(2)}, u32[]{:S(2)}) %collective-permute-start.3) | collective-permute-done | bytes 1048608 | tf_op jit(solution)/shard_map/ppermute | solution.py:21
  127.4 2.8 %gather_fusion.3 = bf16[32,8,2048]{2,1,0:T(8,128)(2,1)} fusion(bf16[32,8,2048]{2,1,0:T(8,128)(2,1)} %collective-permute-done.3, s32[1024]{0:T(1024)S(1)} %pad_clamp_fusion), kind=kCustom, calls=%fused_computation.3.clone | custom fusion | bytes 2097280 | tf_op jit(solution)/shard_map/jit(_take)/gather | solution.py:72
  130.3 1.6 select_convert_fusion
  131.8 0.3 copy-done.1
  132.2 5.4 %add_reduce_fusion.3 = (f32[32,1024]{1,0:T(8,128)S(1)}, f32[32,1024]{1,0:T(8,128)S(1)}, f32[32,1024]{1,0:T(8,128)S(1)}, f32[32,1024]{1,0:T(8,128)S(1)}, f32[32,1...) fusion(f32[32,8,2048]{2,1,0:T(8,128)S(1)} %copy-done.1, ...), kind=kLoop, calls=%fused_computation.52 | loop fusion | flops 8126464 | bytes 11534336 | tf_op jit(solution)/shard_map/reduce_sum | solution.py:52
  137.7 1.1 pad_maximum_fusion
  138.8 0.0 all-gather.3.cloned.1.call-update
  138.8 4.3 %fusion.24 = (f32[1024,257]{0,1:T(8,128)S(1)}, f32[1024,257]{0,1:T(8,128)S(1)}) fusion(s32[257]{0:T(512)S(1)} %add_select_fusion.2), kind=kLoop, calls=%fused_computation.53 | loop fusion | flops 3947520 | bytes 2106372 | tf_op jit(solution)/shard_map/cos | solution.py:39
  143.2 45.3 %all-gather.3.cloned.1.call-done = f32[64,4,2048]{2,0,1:T(8,128)} async-done(((f32[32,4,2048]{2,0,1:T(8,128)}), f32[64,4,2048]{2,0,1:T(8,128)}) %all-gather.3.cloned.1.call-update) | async-done | bytes 2097168 | tf_op jit(solution)/shard_map/all_gather | solution.py:13
  188.5 2.8 %reduce_sum.99 = f32[32,4,2048]{2,0,1:T(8,128)} reduce(f32[2,32,4,2048]{3,1,0,2:T(8,128)} %bitcast.60, f32[]{:T(128)} %constant.52.clone.1), dimensions={0}, to_apply=%region_9.11 | reduce | flops 262144 | bytes 3145732 | tf_op jit(solution)/shard_map/reduce_sum | solution.py:13
  191.3 4.1 %fusion.16 = f32[32,4,257]{2,0,1:T(8,128)S(1)} fusion(f32[32,4,2048]{2,0,1:T(8,128)} %reduce_sum.99, f32[1024,257]{0,1:T(8,128)S(1)} %get-tuple-element.40, f32[1024,257]{0,1:T(8,128)S(1)} %get-tuple-element.39), kind=kOutput, calls=%fused_computation.31 | convolution fusion | flops 809011328 | bytes 3285504 | tf_op jit(solution)/shard_map/dot_general | solution.py:79
  195.4 0.2 reverse
  195.7 0.1 slice_bitcast_fusion.3
  195.8 10.9 %collective-permute-start.7 = (f32[32,257]{1,0:T(8,128)S(1)}, f32[32,257]{1,0:T(8,128)S(1)}, u32[]{:S(2)}, u32[]{:S(2)}) collective-permute-start(f32[32,257]{1,0:T(8,128)S(1)} %slice_bitcast_fusion.3), channel_id=1, source_target_pairs={{0,504},{2,506},{4,508},{6,510},{8,0},{10,2},{12,4},{14,6},{16,8},... | collective-permute-start | bytes 98696 | tf_op jit(solution)/shard_map/ppermute | solution.py:21
  206.6 0.2 reverse.1
  206.9 0.1 slice_bitcast_fusion.2
  206.9 3.9 %collective-permute-start.6 = (f32[32,257]{1,0:T(8,128)S(1)}, f32[32,257]{1,0:T(8,128)S(1)}, u32[]{:S(2)}, u32[]{:S(2)}) collective-permute-start(f32[32,257]{1,0:T(8,128)S(1)} %slice_bitcast_fusion.2), channel_id=1, source_target_pairs={{0,506},{2,508},{4,510},{6,0},{8,2},{10,4},{12,6},{14,8},{16,10},{... | collective-permute-start | bytes 98696 | tf_op jit(solution)/shard_map/ppermute | solution.py:21
  210.8 0.2 reverse.2
  211.1 0.1 slice_bitcast_fusion.1
  211.2 3.1 %collective-permute-start.5 = (f32[32,257]{1,0:T(8,128)S(1)}, f32[32,257]{1,0:T(8,128)S(1)}, u32[]{:S(2)}, u32[]{:S(2)}) collective-permute-start(f32[32,257]{1,0:T(8,128)S(1)} %slice_bitcast_fusion.1), channel_id=1, source_target_pairs={{0,508},{2,510},{4,0},{6,2},{8,4},{10,6},{12,8},{14,10},{16,12},{1... | collective-permute-start | bytes 98696 | tf_op jit(solution)/shard_map/ppermute | solution.py:21
  214.2 0.2 reverse.3
  214.5 0.1 slice_bitcast_fusion
  214.6 1.9 collective-permute-start.4
  216.5 0.8 copy.9
  217.3 0.0 collective-permute-done.7
  217.3 2.7 %collective-permute-done.4 = f32[32,257]{1,0:T(8,128)S(1)} collective-permute-done((f32[32,257]{1,0:T(8,128)S(1)}, f32[32,257]{1,0:T(8,128)S(1)}, u32[]{:S(2)}, u32[]{:S(2)}) %collective-permute-start.4) | collective-permute-done | bytes 32928 | tf_op jit(solution)/shard_map/ppermute | solution.py:21
  220.0 0.8 copy.10
  (22 shorter events, 0.2 us)
Async XLA Ops:
  7.2 33.9 %copy-start = (bf16[32,8,2048]{2,1,0:T(8,128)(2,1)S(1)}, bf16[32,8,2048]{2,1,0:T(8,128)(2,1)}, u32[]{:S(2)}) copy-start(bf16[32,8,2048]{2,1,0:T(8,128)(2,1)} %param.5) | copy-start | bytes 3145732
  7.2 33.9 %copy-start.4 = (s32[32]{0:T(128)S(1)}, s32[32]{0:T(128)}, u32[]{:S(2)}) copy-start(s32[32]{0:T(128)} %param.7) | copy-start | bytes 388
  7.2 181.3 %all-gather.3.cloned.1.call-start = ((), (), s32[]{:S(2)}) async-start(), calls=%async_computation | async-start | bytes 3145728 | tf_op jit(solution)/shard_map/all_gather | solution.py:13
  46.3 39.9 %copy-start.3 = (s32[4,32]{1,0:T(4,128)S(1)}, s32[4,32]{1,0:T(4,128)}, u32[]{:S(2)}) copy-start(s32[4,32]{1,0:T(4,128)} %param.6) | copy-start | bytes 1540
  48.2 16.3 %collective-permute-start = (bf16[32,8,2048]{2,1,0:T(8,128)(2,1)S(1)}, bf16[32,8,2048]{2,1,0:T(8,128)(2,1)S(1)}, u32[]{:S(2)}, u32[]{:S(2)}) collective-permute-start(bf16[32,8,2048]{2,1,0:T(8,128)(2,1)S(1)} %get-tuple-element.28), channel_id=1, source_target_pairs={{0,2},{2,4},{4,6},{6,8},{8,10},{10,12},{12,14},{14,16},{16,18},{18... | collective-permute-start | bytes 3145736 | tf_op jit(solution)/shard_map/ppermute | solution.py:21
  64.6 1.0 copy-start.2
  65.5 17.6 %collective-permute-start.1 = (bf16[32,8,2048]{2,1,0:T(8,128)(2,1)S(1)}, bf16[32,8,2048]{2,1,0:T(8,128)(2,1)}, u32[]{:S(2)}, u32[]{:S(2)}) collective-permute-start(bf16[32,8,2048]{2,1,0:T(8,128)(2,1)S(1)} %collective-permute-done), channel_id=1, source_target_pairs={{0,2},{2,4},{4,6},{6,8},{8,10},{10,12},{12,14},{14,16},{16,18},{18... | collective-permute-start | bytes 3145736 | tf_op jit(solution)/shard_map/ppermute | solution.py:21
  83.1 22.1 %collective-permute-start.2 = (bf16[32,8,2048]{2,1,0:T(8,128)(2,1)}, bf16[32,8,2048]{2,1,0:T(8,128)(2,1)}, u32[]{:S(2)}, u32[]{:S(2)}) collective-permute-start(bf16[32,8,2048]{2,1,0:T(8,128)(2,1)} %collective-permute-done.1), channel_id=1, source_target_pairs={{0,2},{2,4},{4,6},{6,8},{8,10},{10,12},{12,14},{14,16},{16,18},{18... | collective-permute-start | bytes 3145736 | tf_op jit(solution)/shard_map/ppermute | solution.py:21
  105.3 22.1 %collective-permute-start.3 = (bf16[32,8,2048]{2,1,0:T(8,128)(2,1)}, bf16[32,8,2048]{2,1,0:T(8,128)(2,1)}, u32[]{:S(2)}, u32[]{:S(2)}) collective-permute-start(bf16[32,8,2048]{2,1,0:T(8,128)(2,1)} %collective-permute-done.2), channel_id=1, source_target_pairs={{0,2},{2,4},{4,6},{6,8},{8,10},{10,12},{12,14},{14,16},{16,18},{18... | collective-permute-start | bytes 3145736 | tf_op jit(solution)/shard_map/ppermute | solution.py:21
  130.3 1.9 copy-start.1
  195.8 21.5 %collective-permute-start.7 = (f32[32,257]{1,0:T(8,128)S(1)}, f32[32,257]{1,0:T(8,128)S(1)}, u32[]{:S(2)}, u32[]{:S(2)}) collective-permute-start(f32[32,257]{1,0:T(8,128)S(1)} %slice_bitcast_fusion.3), channel_id=1, source_target_pairs={{0,504},{2,506},{4,508},{6,510},{8,0},{10,2},{12,4},{14,6},{16,8},... | collective-permute-start | bytes 98696 | tf_op jit(solution)/shard_map/ppermute | solution.py:21
  206.9 10.4 %collective-permute-start.6 = (f32[32,257]{1,0:T(8,128)S(1)}, f32[32,257]{1,0:T(8,128)S(1)}, u32[]{:S(2)}, u32[]{:S(2)}) collective-permute-start(f32[32,257]{1,0:T(8,128)S(1)} %slice_bitcast_fusion.2), channel_id=1, source_target_pairs={{0,506},{2,508},{4,510},{6,0},{8,2},{10,4},{12,6},{14,8},{16,10},{... | collective-permute-start | bytes 98696 | tf_op jit(solution)/shard_map/ppermute | solution.py:21
  211.2 6.1 %collective-permute-start.5 = (f32[32,257]{1,0:T(8,128)S(1)}, f32[32,257]{1,0:T(8,128)S(1)}, u32[]{:S(2)}, u32[]{:S(2)}) collective-permute-start(f32[32,257]{1,0:T(8,128)S(1)} %slice_bitcast_fusion.1), channel_id=1, source_target_pairs={{0,508},{2,510},{4,0},{6,2},{8,4},{10,6},{12,8},{14,10},{16,12},{1... | collective-permute-start | bytes 98696 | tf_op jit(solution)/shard_map/ppermute | solution.py:21
  214.6 5.4 %collective-permute-start.4 = (f32[32,257]{1,0:T(8,128)S(1)}, f32[32,257]{1,0:T(8,128)S(1)}, u32[]{:S(2)}, u32[]{:S(2)}) collective-permute-start(f32[32,257]{1,0:T(8,128)S(1)} %slice_bitcast_fusion), channel_id=1, source_target_pairs={{0,510},{2,0},{4,2},{6,4},{8,6},{10,8},{12,10},{14,12},{16,14},{18... | collective-permute-start | bytes 98696 | tf_op jit(solution)/shard_map/ppermute | solution.py:21
Sparse Core Ops, SparseCore 0:
  138.9 49.4 all-gather.2
